TPU v7x, 32 devices: a whole 2x2x4 slice. The times are simulated.
32 devices in a mesh: layer: 4 (over x, core), tok: 8 (over z, y).
Axes of the slice: x: 2, y: 2, z: 4, core: 2. Of those that a mesh axis runs over, the one named last changes fastest.
Arguments:
- active_codes: bfloat16 [4, 1024, 32], P('layer', 'tok'), may hold values from 0.19921875 to 3
- latent_ids: int32 [4, 1024, 32], P('layer', 'tok'), may hold values from 0 to 32767, as said below
- decoder: bfloat16 [4, 32768, 4096], P('layer', 'tok'), may hold values from -1 to 1
- carry_gain: float32 [4, 4096], P('layer'), may hold values from 0.1 to 1
- earlier_sum: bfloat16 [1024, 4096], P('tok'), may hold values from -6 to 6
- targets: bfloat16 [4, 1024, 4096], P('layer', 'tok'), may hold values from -6 to 6
Outputs:
- reconstruction: bfloat16 [4, 1024, 4096], P('layer', 'tok')
- code_grad: float32 [4, 1024, 32], P('layer', 'tok')
Inputs may be any that keep to these rules, and one draw needn't show every extreme that they name: `latent_ids`: A token's 32 ids in one layer are distinct. In each layer, the 128 tokens of one aligned block have at most 768 ids in any one range of 4096 consecutive latents, and in every layer one range holds exactly 768 ids of every block.
All inputs are finite; a program needn't handle non-finite values.
Results may differ from a plain program's by a relative error of at most 0.019.
Values may be sent and summed in bfloat16 or wider, within the bound.
No kernel may reach another device: no remote copies, remote signals or barrier semaphores. Data moves between devices by JAX's collectives and lax.ppermute only.
A program may use at most 256 MiB of HBM per device.

v0:
```python
import jax
import jax.numpy as jnp
from jax import lax
from jax.sharding import PartitionSpec as P


def prefix(shard, axis, combine, identity, reverse):
    length, mine = (lax.axis_size(axis), lax.axis_index(axis))
    everything = jax.tree.map(
        lambda part, kind: lax.all_gather(part.astype(kind), axis),
        shard,
        (jnp.bfloat16, jnp.bfloat16),
    )
    start = jax.tree.map(
        lambda part, zero: jnp.broadcast_to(jnp.asarray(zero, part.dtype), part.shape),
        shard,
        identity,
    )

    def lap(k, before):
        at = length - 1 - k if reverse else k
        reached = at > mine if reverse else at < mine
        new = combine(
            before, jax.tree.map(lambda part, own: part[at].astype(own.dtype), everything, shard)
        )
        return jax.tree.map(lambda a, b: jnp.where(reached, a, b), new, before)

    return lax.fori_loop(0, length, lap, start)


def bucket_lists(latent_rows, code_rows, range_size, owners, capacity):
    tok_rows, top_count = latent_rows.shape
    entries = tok_rows * top_count
    flat_ids = latent_rows.reshape(entries)
    owning = flat_ids // range_size
    within = flat_ids % range_size
    positions = jnp.arange(entries, dtype=jnp.int32) // top_count
    ordering = jnp.argsort(owning, stable=True)
    counts = jnp.sum(
        (owning[:, None] == jnp.arange(owners, dtype=jnp.int32)[None, :]).astype(jnp.int32), axis=0
    )
    starts = jnp.cumsum(counts) - counts
    sorted_rank = jnp.arange(entries, dtype=jnp.int32) - starts[owning[ordering]]
    rank_of = jnp.zeros(entries, jnp.int32).at[ordering].set(sorted_rank)
    slot_index = owning * capacity + rank_of
    slot_keys = (
        jnp.zeros(owners * capacity, jnp.int32).at[slot_index].set(within * tok_rows + positions)
    )
    slot_codes = (
        jnp.zeros(owners * capacity, jnp.bfloat16).at[slot_index].set(code_rows.reshape(entries))
    )
    return (slot_keys.reshape(owners, capacity), slot_codes.reshape(owners, capacity), slot_index)


def source_term(rows, slot_keys, slot_codes, tok_rows):
    token_index = slot_keys % tok_rows
    matches = token_index[None, :] == jnp.arange(tok_rows, dtype=jnp.int32)[:, None]
    spread = jnp.where(matches, slot_codes[None, :], jnp.zeros((), jnp.bfloat16))
    return jnp.dot(spread, rows, preferred_element_type=jnp.float32)


def slot_grads_of(rows, slot_keys, grad_block, tok_rows):
    token_index = slot_keys % tok_rows
    products = jnp.einsum("td,cd->tc", grad_block, rows, preferred_element_type=jnp.float32)
    matches = token_index[None, :] == jnp.arange(tok_rows, dtype=jnp.int32)[:, None]
    return jnp.sum(jnp.where(matches, products, 0.0), axis=0)


def compose(earlier_part, later_part):
    return (earlier_part[0] * later_part[0], later_part[0] * earlier_part[1] + later_part[1])


def on_device(active_codes, latent_ids, decoder, carry_gain, earlier_sum, targets):
    owners = lax.axis_size("tok")
    tok_rows = active_codes.shape[1]
    top_count = active_codes.shape[2]
    range_size = decoder.shape[1]
    model_width = decoder.shape[2]
    capacity = 3 * tok_rows * top_count // (2 * owners)
    weights = decoder[0]
    slot_keys, slot_codes, slot_index = bucket_lists(
        latent_ids[0], active_codes[0], range_size, owners, capacity
    )
    recv_keys, recv_codes = (
        lax.all_to_all(slot_keys, "tok", split_axis=0, concat_axis=0, tiled=True),
        lax.all_to_all(slot_codes, "tok", split_axis=0, concat_axis=0, tiled=True),
    )
    row_cache = jnp.take(weights, recv_keys // tok_rows, axis=0)

    def one_source(triple):
        return source_term(triple[2], triple[0], triple[1], tok_rows)

    keys_part = recv_keys
    rows_part = row_cache
    term_blocks = lax.map(one_source, (keys_part, recv_codes, rows_part))
    decoded = lax.psum_scatter(
        term_blocks.reshape(lax.axis_size("tok") * tok_rows, model_width).astype(jnp.bfloat16),
        "tok",
        scatter_dimension=0,
        tiled=True,
    ).astype(jnp.float32)
    identity = (jnp.ones_like(carry_gain), jnp.zeros_like(decoded))
    ahead_gain, ahead_sum = prefix((carry_gain, decoded), "layer", compose, identity, False)
    recon_full = carry_gain * (ahead_gain * earlier_sum.astype(jnp.float32) + ahead_sum) + decoded
    misfit = recon_full - targets[0].astype(jnp.float32)
    behind_gain, behind_sum = prefix(
        (carry_gain, carry_gain * misfit), "layer", compose, identity, True
    )
    grad_low = (misfit + behind_sum).astype(jnp.bfloat16)

    def grads_of_source(triple):
        return slot_grads_of(triple[2], triple[0], triple[1], tok_rows)

    segment = lax.all_gather(grad_low, "tok", axis=0, tiled=True)
    source_count = segment.shape[0] // tok_rows
    keys_part = recv_keys
    rows_part = row_cache
    grad_blocks = segment.reshape(source_count, tok_rows, model_width)
    values = lax.map(grads_of_source, (keys_part, grad_blocks, rows_part))
    returned = lax.all_to_all(values, "tok", split_axis=0, concat_axis=0, tiled=True)
    code_grad = jnp.take(returned.reshape(owners * capacity), slot_index).reshape(
        tok_rows, top_count
    )
    return (recon_full.astype(jnp.bfloat16)[None], code_grad[None])


def solution(mesh):
    return jax.shard_map(
        on_device,
        mesh=mesh,
        in_specs=(
            P("layer", "tok", None),
            P("layer", "tok", None),
            P("layer", "tok", None),
            P("layer", None),
            P("tok", None),
            P("layer", "tok", None),
        ),
        out_specs=(P("layer", "tok", None), P("layer", "tok", None)),
        check_vma=False,
    )
```

profile of v0, /device:TPU:0, one launch (start us, length us, event | category | flops | bytes accessed | tf_op | source)
XLA Modules:
  0.0 932.6 jit_solution(17020449953633308792)
XLA Ops:
  9.1 5.8 sort.17
  14.9 23.0 %gather_fusion = s32[4096]{0:T(1024)S(1)} fusion(s32[4096]{0:T(1024)S(1)} %add_select_fusion.3, s32[4096]{0:T(1024)S(1)} %get-tuple-element.481), kind=kCustom, calls=%fused_computation | custom fusion | bytes 49152 | tf_op jit(solution)/shard_map/gather | solution.py:43
  43.0 15.5 %scatter_custom_fusion = s32[4096]{0:T(1024)S(1)} fusion(s32[4096]{0:T(1024)S(1)} %get-tuple-element.482, s32[4096]{0:T(1024)S(1)} %select_subtract_fusion, s32[]{:T(128)} %constant.237.clone.1), kind=kCustom, calls=%fused_computation.106 | custom fusion | bytes 16388 | tf_op jit(solution)/shard_map/scatter | solution.py:44
  59.4 28.6 %scatter_custom_fusion.2 = bf16[6144]{0:T(1024)(128)(2,1)S(1)} fusion(s32[4096]{0:T(1024)S(1)} %get-tuple-element.475, bf16[4096]{0:T(1024)(128)(2,1)S(1)} %reshape.307, bf16[]{:T(256)} %constant.252.clone.1), kind=kCustom, calls=%fused_computation.108 | custom fusion | bytes 12290 | tf_op jit(solution)/shard_map/scatter | solution.py:50
  89.9 7.3 all-to-all-start.1
  97.1 16.1 %scatter_custom_fusion.1 = s32[6144]{0:T(1024)} fusion(s32[4096]{0:T(1024)S(1)} %get-tuple-element.475, s32[4096]{0:T(1024)S(1)} %get-tuple-element.480, s32[]{:T(128)} %constant.237.clone.1), kind=kCustom, calls=%fused_computation.101 | custom fusion | bytes 24580 | tf_op jit(solution)/shard_map/scatter | solution.py:47
  113.2 6.0 all-to-all-start
  120.1 5.8 all-to-all-done
  126.0 262.2 %gather_fusion.1 = bf16[6144,4096]{1,0:T(8,128)(2,1)} fusion(bf16[4096,4096]{1,0:T(8,128)(2,1)} %bitcast.100, s32[6144]{0:T(1024)S(1)} %broadcast_clamp_fusion), kind=kCustom, calls=%fused_computation.1 | custom fusion | bytes 100687872 | tf_op jit(solution)/shard_map/jit(_take)/gather | solution.py:88
  388.3 33.4 %broadcast_select_fusion.2 = bf16[8,768,4096]{2,1,0:T(8,128)(2,1)} fusion(bf16[8,768,4096]{2,1,0:T(8,128)(2,1)} %bitcast.101, pred[8,768]{1,0:T(8,128)(4,1)S(1)} %compare_and_fusion), kind=kLoop, calls=%fused_computation.46 | loop fusion | flops 25165824 | bytes 100669440 | tf_op jit(solution)/shard_map/jit(_take)/select_n | solution.py:88
  421.7 44.3 %while.56 = (s32[]{:T(128)}, bf16[8,128,4096]{2,1,0:T(8,128)(2,1)}, s32[8,768]{1,0:T(8,128)S(1)}, bf16[8,768]{1,0:T(8,128)(2,1)}, bf16[8,768,4096]{2,1,0:T(8,128)(2,1)}, /*index=5*/s32[]{:T(128)}) while((s32[]{:T(128)}, bf16[8,128,4096]{2,1,0:T(8,128)(2,1)}, s32[8,768]{1,0:T(8,128)S(1)}, bf16[8,768]{1,0:T(8,128)(2,1)}, ...), condition=%wide.region_7.8_spmd, body=%wide.region_6.7_spmd.sunk | while | flops 805511424 | bytes 8403533 | solution.py:95
  433.5 4.8 fusion.63
  450.1 4.8 fusion.63
  461.2 4.8 fusion.63
  466.0 159.1 %reduce-scatter.2.cloned.1.call-done = bf16[128,4096]{1,0:T(8,128)(2,1)} async-done(((bf16[1024,4096]{1,0:T(8,128)(2,1)}), bf16[128,4096]{1,0:T(8,128)(2,1)}) %reduce-scatter.2.cloned.1.call-update) | async-done | bytes 1048592 | tf_op jit(solution)/shard_map/reduce_scatter | solution.py:96
  625.2 5.2 all-gather.3
  630.5 29.8 %all-gather.10.cloned.1.call-done = bf16[512,4096]{1,0:T(8,128)(2,1)} async-done(((bf16[128,4096]{1,0:T(8,128)(2,1)}), bf16[512,4096]{1,0:T(8,128)(2,1)}) %all-gather.10.cloned.1.call-update) | async-done | bytes 4194320 | tf_op jit(solution)/shard_map/all_gather | solution.py:10
  660.2 10.5 %while.58 = (s32[]{:T(128)}, f32[1,4096]{1,0:T(1,128)S(1)}, f32[128,4096]{1,0:T(8,128)S(1)}, s32[]{:T(128)}, bf16[4,1,4096]{2,1,0:T(2,128)(2,1)S(1)}, /*index=5*/bf16[4,128,4096]{2,1,0:T(8,128)(2,1)}, s32[]{:T(128)}, s32[]{:T(128)}) while((s32[]{:T(128)}, f32[1,4096]{1,0:T(1,128)S(1)}, f32[128,4096]{1,0:T(8,128)S(1)}, ...), condition=%wide.region_10.11_spmd.clone, body=%wide.region_9.10_spmd.clone.sunk | while | flops 2637828 | bytes 5316723 | solution.py:28
  674.8 34.6 %all-gather.12.cloned.1.call-done = bf16[512,4096]{1,0:T(8,128)(2,1)} async-done(((bf16[128,4096]{1,0:T(8,128)(2,1)}), bf16[512,4096]{1,0:T(8,128)(2,1)}) %all-gather.12.cloned.1.call-update) | async-done | bytes 4194320 | tf_op jit(solution)/shard_map/all_gather | solution.py:10
  709.3 10.4 %while.59 = (s32[]{:T(128)}, f32[128,4096]{1,0:T(8,128)S(1)}, s32[]{:T(128)}, bf16[4,1,4096]{2,1,0:T(2,128)(2,1)S(1)}, bf16[4,128,4096]{2,1,0:T(8,128)(2,1)}, /*index=5*/s32[]{:T(128)}, s32[]{:T(128)}, s32[]{:T(128)}, s32[]{:T(128)}) while((s32[]{:T(128)}, f32[128,4096]{1,0:T(8,128)S(1)}, s32[]{:T(128)}, ...), condition=%wide.region_12.13_spmd.clone, body=%wide.region_11.12_spmd.clone.sunk | while | flops 2625544 | bytes 5284007 | solution.py:28
  723.9 125.1 %all-gather.8.cloned.1.call-done = bf16[1024,4096]{1,0:T(8,128)(2,1)} async-done(((bf16[128,4096]{1,0:T(8,128)(2,1)}), bf16[1024,4096]{1,0:T(8,128)(2,1)}) %all-gather.8.cloned.1.call-update) | async-done | bytes 8388624 | tf_op jit(solution)/shard_map/all_gather | solution.py:114
  849.0 44.0 %while.57 = (s32[]{:T(128)}, f32[8,768]{1,0:T(8,128)S(1)}, s32[8,768]{1,0:T(8,128)S(1)}, bf16[8,128,4096]{2,1,0:T(8,128)(2,1)}, bf16[8,768,4096]{2,1,0:T(8,128)(2,1)}, /*index=5*/s32[]{:T(128)}, s32[]{:T(128)}) while((s32[]{:T(128)}, f32[8,768]{1,0:T(8,128)S(1)}, s32[8,768]{1,0:T(8,128)S(1)}, bf16[8,128,4096]{2,1,0:T(8,128)(2,1)}, ...), condition=%wide.region_15.16_spmd, body=%wide.region_13.15_spmd.sunk | while | flops 805608960 | bytes 7365717 | solution.py:119
  849.0 5.3 fusion.67
  854.5 5.3 fusion.67
  860.0 5.3 fusion.67
  865.5 5.3 fusion.67
  871.0 5.3 fusion.67
  876.5 5.3 fusion.67
  882.0 5.3 fusion.67
  887.6 5.3 fusion.67
  893.0 9.2 all_to_all.37
  902.3 23.0 %gather_fusion.2 = f32[4096]{0:T(1024)S(1)} fusion(f32[6144]{0:T(1024)S(1)} %bitcast.99, s32[4096]{0:T(1024)S(1)} %copy-done.4), kind=kCustom, calls=%fused_computation.2 | custom fusion | bytes 49152 | tf_op jit(solution)/shard_map/jit(_take)/gather | solution.py:121
  (119 shorter events, 71.2 us)
Async XLA Ops:
  14.9 44.3 %copy-start.5 = (bf16[1,128,32]{1,2,0:T(8,128)(2,1)S(1)}, bf16[1,128,32]{1,2,0:T(8,128)(2,1)}, u32[]{:S(2)}) copy-start(bf16[1,128,32]{1,2,0:T(8,128)(2,1)} %param.14) | copy-start | bytes 24580
  59.2 60.3 %copy-start.2 = (s32[4096]{0:T(1024)}, s32[4096]{0:T(1024)S(1)}, u32[]{:S(2)}) copy-start(s32[4096]{0:T(1024)S(1)} %get-tuple-element.475) | copy-start | bytes 49156
  89.9 23.4 %all-to-all-start.1 = ((bf16[8,2,384]{2,1,0:T(2,128)(2,1)}), bf16[8,2,384]{2,1,0:T(2,128)(2,1)S(1)}, u32[]{:S(2)}, u32[]{:S(2)}) async-start(bf16[8,2,384]{2,1,0:T(2,128)(2,1)} %reshape.367), calls=%async_computation.1 | async-start | bytes 24576 | tf_op jit(solution)/shard_map/all_to_all | solution.py:86
  113.2 12.6 %all-to-all-start = ((s32[8,1,768]{2,1,0:T(1,128)}), s32[8,1,768]{2,1,0:T(1,128)S(1)}, u32[]{:S(2)}, u32[]{:S(2)}) async-start(s32[8,1,768]{2,1,0:T(1,128)} %bitcast.18), calls=%async_computation | async-start | bytes 49152 | tf_op jit(solution)/shard_map/all_to_all | solution.py:85
  119.2 505.9 %reduce-scatter.2.cloned.1.call-start = ((), (), s32[]{:S(2)}) async-start(), calls=%async_computation.4 | async-start | bytes 9437184 | tf_op jit(solution)/shard_map/reduce_scatter | solution.py:96
  466.0 159.2 %copy-start.1 = (f32[1,4096]{1,0:T(1,128)S(1)}, f32[1,4096]{1,0:T(1,128)}, u32[]{:S(2)}) copy-start(f32[1,4096]{1,0:T(1,128)} %param.17) | copy-start | bytes 49156
  466.0 194.3 %all-gather.10.cloned.1.call-start = ((), (), s32[]{:S(2)}) async-start(), calls=%async_computation.6 | async-start | bytes 5242880 | tf_op jit(solution)/shard_map/all_gather | solution.py:10
  625.1 84.2 %all-gather.12.cloned.1.call-start = ((), (), s32[]{:S(2)}) async-start(), calls=%async_computation.7 | async-start | bytes 5242880 | tf_op jit(solution)/shard_map/all_gather | solution.py:10
  660.2 10.6 %copy-start = (bf16[1,128,4096]{2,1,0:T(8,128)(2,1)S(1)}, bf16[1,128,4096]{2,1,0:T(8,128)(2,1)}, u32[]{:S(2)}) copy-start(bf16[1,128,4096]{2,1,0:T(8,128)(2,1)} %param.19) | copy-start | bytes 3145732
  674.7 174.3 %all-gather.8.cloned.1.call-start = ((), (), s32[]{:S(2)}) async-start(), calls=%async_computation.5 | async-start | bytes 9437184 | tf_op jit(solution)/shard_map/all_gather | solution.py:114
  849.0 53.3 %copy-start.4 = (s32[4096]{0:T(1024)S(1)}, s32[4096]{0:T(1024)}, u32[]{:S(2)}) copy-start(s32[4096]{0:T(1024)} %get-tuple-element.474) | copy-start | bytes 49156
  902.3 23.0 %copy-start.3 = (s32[4096]{0:T(1024)S(1)}, s32[4096]{0:T(1024)}, u32[]{:S(2)}) copy-start(s32[4096]{0:T(1024)} %copy-done.2) | copy-start | bytes 49156
Sparse Core Ops, SparseCore 0:
  466.1 158.9 reduce-scatter.1
  626.7 33.4 all-gather.9
  674.8 34.4 all-gather.11
  724.0 124.9 all-gather.7
where the time goes:
time: 940 us; the launch traced here: 933 us
  local copies, waits for them, and re-layouts  379 us (40%)
  waiting for transfers between devices  354 us (38%)
  matrix products  80.9 us (9%)
  other arithmetic  75.3 us (8%)
  blocking collectives  14.5 us (2%)
  between operations  14 us (1%)
  starting transfers between devices  13.6 us (1%)
    gather x1, local copies, waits for them, and re-layouts, on_device(): row_cache = jnp.take(weights, recv_keys // tok_rows, axis=0)  262 us
    reduce_scatter x1, waiting for transfers between devices, on_device(): lax.psum_scatter(term_blocks.reshape(lax.axis_size('tok') * tok_rows, mod...  159 us
    all_gather x1, waiting for transfers between devices, on_device(): segment = lax.all_gather(grad_low, 'tok', axis=0, tiled=True)  125 us
    all_gather x2, waiting for transfers between devices, prefix(): lax.all_gather(part.astype(kind), axis)  64.4 us
    dot_general x8, matrix products, slot_grads_of(): jnp.einsum('td,cd->tc', grad_block, rows, preferred_element_type=jnp.floa...  42.8 us
    dot_general x8, matrix products, source_term(): return jnp.dot(spread, rows, preferred_element_type=jnp.float32)  38.1 us
    select_n x2, other arithmetic, on_device(): row_cache = jnp.take(weights, recv_keys // tok_rows, axis=0)  33.5 us
    scatter x1, local copies, waits for them, and re-layouts, bucket_lists(): jnp.zeros(owners * capacity, jnp.bfloat16).at[slot_index]  28.6 us
  transfers between devices with their start and end apart: 6, of which 5 were waited for; matrix products, arithmetic and copies ran while one was open for 2% of the time, Pallas kernels for 0%

commit v1 on v0

--- a/solution.py
+++ b/solution.py
@@ -111,7 +111,14 @@
     def grads_of_source(triple):
         return slot_grads_of(triple[2], triple[0], triple[1], tok_rows)
 
-    segment = lax.all_gather(grad_low, "tok", axis=0, tiled=True)
+    carry_out, part_now = (lax.axis_size("tok"), lax.axis_index("tok"))
+    segment, res = (grad_low, 1)
+    while res < carry_out:
+        r2 = lax.ppermute(segment, "tok", [(m, m ^ res) for m in range(carry_out)])
+        found_now = jnp.concatenate([segment, r2], axis=0)
+        out_arr = jnp.concatenate([r2, segment], axis=0)
+        segment = jnp.where(part_now & res == 0, found_now, out_arr)
+        res = 2 * res
     source_count = segment.shape[0] // tok_rows
     keys_part = recv_keys
     rows_part = row_cache

time: 940 us -> 1090 us (1.16)
  waiting for transfers between devices: 354 us -> 478 us
  other arithmetic: 75.3 us -> 93 us
    ppermute x0 -> x3, waiting for transfers between devices: none -> 249 us  [on_device(): r2 = lax.ppermute(segment, 'tok', [(m, m ^ res) for m in range(carry_out)])]
    all_gather x1 -> x0, waiting for transfers between devices: 125 us -> none  [on_device(): segment = lax.all_gather(grad_low, 'tok', axis=0, tiled=True)]
    select_n x0 -> x3, other arithmetic: none -> 17.8 us  [on_device(): segment = jnp.where(part_now & res == 0, found_now, out_arr)]
  transfers between devices with their start and end apart: 6 -> 8, of which waited for: 5 -> 7; matrix products, arithmetic and copies ran while one was open for 2% -> 2% of each run, Pallas kernels for 0% -> 0%
where the time goes in v1:
time: 1090 us; the launch traced here: 1080 us
  waiting for transfers between devices  478 us (44%)
  local copies, waits for them, and re-layouts  379 us (35%)
  other arithmetic  93 us (9%)
  matrix products  80.9 us (7%)
  starting transfers between devices  19 us (2%)
  blocking collectives  17.2 us (2%)
  between operations  14 us (1%)
    gather x1, local copies, waits for them, and re-layouts, on_device(): row_cache = jnp.take(weights, recv_keys // tok_rows, axis=0)  262 us
    ppermute x3, waiting for transfers between devices, on_device(): r2 = lax.ppermute(segment, 'tok', [(m, m ^ res) for m in range(carry_out)])  249 us
    reduce_scatter x1, waiting for transfers between devices, on_device(): lax.psum_scatter(term_blocks.reshape(lax.axis_size('tok') * tok_rows, mod...  159 us
    all_gather x2, waiting for transfers between devices, prefix(): lax.all_gather(part.astype(kind), axis)  64.4 us
    dot_general x8, matrix products, slot_grads_of(): jnp.einsum('td,cd->tc', grad_block, rows, preferred_element_type=jnp.floa...  42.8 us
    dot_general x8, matrix products, source_term(): return jnp.dot(spread, rows, preferred_element_type=jnp.float32)  38.1 us
    select_n x2, other arithmetic, on_device(): row_cache = jnp.take(weights, recv_keys // tok_rows, axis=0)  33.5 us
    scatter x1, local copies, waits for them, and re-layouts, bucket_lists(): jnp.zeros(owners * capacity, jnp.bfloat16).at[slot_index]  28.6 us
  transfers between devices with their start and end apart: 8, of which 7 were waited for; matrix products, arithmetic and copies ran while one was open for 2% of the time, Pallas kernels for 0%

profile of v1, /device:TPU:0, one launch (start us, length us, event | category | flops | bytes accessed | tf_op | source)
XLA Modules:
  0.0 1082.6 jit_solution(16874490248339815755)
XLA Ops:
  9.1 5.8 sort.17
  14.9 23.0 %gather_fusion = s32[4096]{0:T(1024)S(1)} fusion(s32[4096]{0:T(1024)S(1)} %add_select_fusion.3, s32[4096]{0:T(1024)S(1)} %get-tuple-element.481), kind=kCustom, calls=%fused_computation | custom fusion | bytes 49152 | tf_op jit(solution)/shard_map/gather | solution.py:43
  43.0 15.5 %scatter_custom_fusion = s32[4096]{0:T(1024)S(1)} fusion(s32[4096]{0:T(1024)S(1)} %get-tuple-element.482, s32[4096]{0:T(1024)S(1)} %select_subtract_fusion, s32[]{:T(128)} %constant.242.clone.1), kind=kCustom, calls=%fused_computation.109 | custom fusion | bytes 16388 | tf_op jit(solution)/shard_map/scatter | solution.py:44
  59.4 28.6 %scatter_custom_fusion.2 = bf16[6144]{0:T(1024)(128)(2,1)S(1)} fusion(s32[4096]{0:T(1024)S(1)} %get-tuple-element.475, bf16[4096]{0:T(1024)(128)(2,1)S(1)} %reshape.308, bf16[]{:T(256)} %constant.257.clone.1), kind=kCustom, calls=%fused_computation.111 | custom fusion | bytes 12290 | tf_op jit(solution)/shard_map/scatter | solution.py:50
  89.9 7.3 all-to-all-start.1
  97.1 16.1 %scatter_custom_fusion.1 = s32[6144]{0:T(1024)} fusion(s32[4096]{0:T(1024)S(1)} %get-tuple-element.475, s32[4096]{0:T(1024)S(1)} %get-tuple-element.480, s32[]{:T(128)} %constant.242.clone.1), kind=kCustom, calls=%fused_computation.104 | custom fusion | bytes 24580 | tf_op jit(solution)/shard_map/scatter | solution.py:47
  113.2 6.0 all-to-all-start
  120.1 5.8 all-to-all-done
  126.0 262.2 %gather_fusion.1 = bf16[6144,4096]{1,0:T(8,128)(2,1)} fusion(bf16[4096,4096]{1,0:T(8,128)(2,1)} %bitcast.100, s32[6144]{0:T(1024)S(1)} %broadcast_clamp_fusion), kind=kCustom, calls=%fused_computation.1 | custom fusion | bytes 100687872 | tf_op jit(solution)/shard_map/jit(_take)/gather | solution.py:88
  388.3 33.4 %broadcast_select_fusion.2 = bf16[8,768,4096]{2,1,0:T(8,128)(2,1)} fusion(bf16[8,768,4096]{2,1,0:T(8,128)(2,1)} %bitcast.101, pred[8,768]{1,0:T(8,128)(4,1)S(1)} %compare_and_fusion), kind=kLoop, calls=%fused_computation.46 | loop fusion | flops 25165824 | bytes 100669440 | tf_op jit(solution)/shard_map/jit(_take)/select_n | solution.py:88
  421.7 44.3 %while.56 = (s32[]{:T(128)}, bf16[8,128,4096]{2,1,0:T(8,128)(2,1)}, s32[8,768]{1,0:T(8,128)S(1)}, bf16[8,768]{1,0:T(8,128)(2,1)}, bf16[8,768,4096]{2,1,0:T(8,128)(2,1)}, /*index=5*/s32[]{:T(128)}) while((s32[]{:T(128)}, bf16[8,128,4096]{2,1,0:T(8,128)(2,1)}, s32[8,768]{1,0:T(8,128)S(1)}, bf16[8,768]{1,0:T(8,128)(2,1)}, ...), condition=%wide.region_7.8_spmd, body=%wide.region_6.7_spmd.sunk | while | flops 805511424 | bytes 8403533 | solution.py:95
  466.0 159.1 %reduce-scatter.2.cloned.1.call-done = bf16[128,4096]{1,0:T(8,128)(2,1)} async-done(((bf16[1024,4096]{1,0:T(8,128)(2,1)}), bf16[128,4096]{1,0:T(8,128)(2,1)}) %reduce-scatter.2.cloned.1.call-update) | async-done | bytes 1048592 | tf_op jit(solution)/shard_map/reduce_scatter | solution.py:96
  625.2 5.2 all-gather.3
  630.5 29.8 %all-gather.7.cloned.1.call-done = bf16[512,4096]{1,0:T(8,128)(2,1)} async-done(((bf16[128,4096]{1,0:T(8,128)(2,1)}), bf16[512,4096]{1,0:T(8,128)(2,1)}) %all-gather.7.cloned.1.call-update) | async-done | bytes 4194320 | tf_op jit(solution)/shard_map/all_gather | solution.py:10
  660.2 10.5 while.58
  674.7 34.6 %all-gather.9.cloned.1.call-done = bf16[512,4096]{1,0:T(8,128)(2,1)} async-done(((bf16[128,4096]{1,0:T(8,128)(2,1)}), bf16[512,4096]{1,0:T(8,128)(2,1)}) %all-gather.9.cloned.1.call-update) | async-done | bytes 4194320 | tf_op jit(solution)/shard_map/all_gather | solution.py:10
  709.3 10.4 while.59
  725.2 23.9 %collective-permute-done = bf16[128,4096]{1,0:T(8,128)(2,1)} collective-permute-done((bf16[128,4096]{1,0:T(8,128)(2,1)S(1)}, bf16[128,4096]{1,0:T(8,128)(2,1)}, u32[]{:S(2)}, u32[]{:S(2)}) %collective-permute-start) | collective-permute-done | bytes 1048608 | tf_op jit(solution)/shard_map/ppermute | solution.py:117
  753.0 45.6 %collective-permute-done.1 = bf16[256,4096]{1,0:T(8,128)(2,1)} collective-permute-done((bf16[256,4096]{1,0:T(8,128)(2,1)S(1)}, bf16[256,4096]{1,0:T(8,128)(2,1)}, u32[]{:S(2)}, u32[]{:S(2)}) %collective-permute-start.1) | collective-permute-done | bytes 2097184 | tf_op jit(solution)/shard_map/ppermute | solution.py:117
  805.6 179.7 %collective-permute-done.2 = bf16[512,4096]{1,0:T(8,128)(2,1)} collective-permute-done((bf16[512,4096]{1,0:T(8,128)(2,1)}, bf16[512,4096]{1,0:T(8,128)(2,1)}, u32[]{:S(2)}, u32[]{:S(2)}) %collective-permute-start.2) | collective-permute-done | bytes 4194336 | tf_op jit(solution)/shard_map/ppermute | solution.py:117
  985.3 10.9 %maximum_select_fusion = bf16[1024,4096]{1,0:T(8,128)(2,1)} fusion(bf16[512,4096]{1,0:T(8,128)(2,1)} %collective-permute-done.2, bf16[512,4096]{1,0:T(8,128)(2,1)} %maximum_select_fusion.1, pred[]{:T(512)S(6)} %eq.82), kind=kLoop, calls=%fused_computation.47 | loop fusion | flops 37748736 | bytes 16777216 | tf_op jit(solution)/shard_map/jit(_where)/select_n | solution.py:120
  996.2 44.0 %while.57 = (s32[]{:T(128)}, f32[8,768]{1,0:T(8,128)S(1)}, s32[8,768]{1,0:T(8,128)S(1)}, bf16[8,128,4096]{2,1,0:T(8,128)(2,1)}, bf16[8,768,4096]{2,1,0:T(8,128)(2,1)}, /*index=5*/s32[]{:T(128)}, s32[]{:T(128)}) while((s32[]{:T(128)}, f32[8,768]{1,0:T(8,128)S(1)}, s32[8,768]{1,0:T(8,128)S(1)}, bf16[8,128,4096]{2,1,0:T(8,128)(2,1)}, ...), condition=%wide.region_15.16_spmd, body=%wide.region_13.15_spmd.sunk | while | flops 805608960 | bytes 7365717 | solution.py:126
  996.2 5.3 fusion.67
  1001.8 5.3 fusion.67
  1007.3 5.3 fusion.67
  1012.8 5.3 fusion.67
  1018.3 5.3 fusion.67
  1023.8 5.3 fusion.67
  1029.3 5.3 fusion.67
  1034.8 5.3 fusion.67
  1040.3 11.9 %all_to_all.37 = f32[8,1,768]{2,1,0:T(1,128)S(1)} all-to-all(f32[8,1,768]{2,1,0:T(1,128)S(1)} %all_to_all.31), channel_id=1, replica_groups=mesh['layer'=4,'tok'=8] {'tok'}, dimensions={0} | all-to-all | bytes 49152 | tf_op jit(solution)/shard_map/all_to_all | solution.py:127
  1052.2 23.0 %gather_fusion.2 = f32[4096]{0:T(1024)S(1)} fusion(f32[6144]{0:T(1024)S(1)} %bitcast.99, s32[4096]{0:T(1024)S(1)} %copy-done.4), kind=kCustom, calls=%fused_computation.2 | custom fusion | bytes 49152 | tf_op jit(solution)/shard_map/jit(_take)/gather | solution.py:128
  (125 shorter events, 97.8 us)
Async XLA Ops:
  14.9 44.3 %copy-start.5 = (bf16[1,128,32]{1,2,0:T(8,128)(2,1)S(1)}, bf16[1,128,32]{1,2,0:T(8,128)(2,1)}, u32[]{:S(2)}) copy-start(bf16[1,128,32]{1,2,0:T(8,128)(2,1)} %param.14) | copy-start | bytes 24580
  59.2 60.3 %copy-start.2 = (s32[4096]{0:T(1024)}, s32[4096]{0:T(1024)S(1)}, u32[]{:S(2)}) copy-start(s32[4096]{0:T(1024)S(1)} %get-tuple-element.475) | copy-start | bytes 49156
  89.9 23.4 %all-to-all-start.1 = ((bf16[8,2,384]{2,1,0:T(2,128)(2,1)}), bf16[8,2,384]{2,1,0:T(2,128)(2,1)S(1)}, u32[]{:S(2)}, u32[]{:S(2)}) async-start(bf16[8,2,384]{2,1,0:T(2,128)(2,1)} %reshape.368), calls=%async_computation.1 | async-start | bytes 24576 | tf_op jit(solution)/shard_map/all_to_all | solution.py:86
  113.2 12.6 %all-to-all-start = ((s32[8,1,768]{2,1,0:T(1,128)}), s32[8,1,768]{2,1,0:T(1,128)S(1)}, u32[]{:S(2)}, u32[]{:S(2)}) async-start(s32[8,1,768]{2,1,0:T(1,128)} %bitcast.18), calls=%async_computation | async-start | bytes 49152 | tf_op jit(solution)/shard_map/all_to_all | solution.py:85
  119.2 505.9 %reduce-scatter.2.cloned.1.call-start = ((), (), s32[]{:S(2)}) async-start(), calls=%async_computation.4 | async-start | bytes 9437184 | tf_op jit(solution)/shard_map/reduce_scatter | solution.py:96
  466.0 159.2 %copy-start.1 = (f32[1,4096]{1,0:T(1,128)S(1)}, f32[1,4096]{1,0:T(1,128)}, u32[]{:S(2)}) copy-start(f32[1,4096]{1,0:T(1,128)} %param.17) | copy-start | bytes 49156
  466.0 194.3 %all-gather.7.cloned.1.call-start = ((), (), s32[]{:S(2)}) async-start(), calls=%async_computation.5 | async-start | bytes 5242880 | tf_op jit(solution)/shard_map/all_gather | solution.py:10
  625.1 84.2 %all-gather.9.cloned.1.call-start = ((), (), s32[]{:S(2)}) async-start(), calls=%async_computation.6 | async-start | bytes 5242880 | tf_op jit(solution)/shard_map/all_gather | solution.py:10
  660.2 10.6 copy-start
  723.7 25.4 %collective-permute-start = (bf16[128,4096]{1,0:T(8,128)(2,1)S(1)}, bf16[128,4096]{1,0:T(8,128)(2,1)}, u32[]{:S(2)}, u32[]{:S(2)}) collective-permute-start(bf16[128,4096]{1,0:T(8,128)(2,1)S(1)} %get-tuple-element.478), channel_id=1, source_target_pairs={{0,1},{1,0},{2,3},{3,2},{4,5},{5,4},{6,7},{7,6},{8,9},{9,8},{10,11... | collective-permute-start | bytes 3145736 | tf_op jit(solution)/shard_map/ppermute | solution.py:117
  751.4 47.1 %collective-permute-start.1 = (bf16[256,4096]{1,0:T(8,128)(2,1)S(1)}, bf16[256,4096]{1,0:T(8,128)(2,1)}, u32[]{:S(2)}, u32[]{:S(2)}) collective-permute-start(bf16[256,4096]{1,0:T(8,128)(2,1)S(1)} %maximum_select_fusion.2), channel_id=1, source_target_pairs={{0,2},{1,3},{2,0},{3,1},{4,6},{5,7},{6,4},{7,5},{8,10},{9,11},{10,... | collective-permute-start | bytes 6291464 | tf_op jit(solution)/shard_map/ppermute | solution.py:117
  803.2 182.1 %collective-permute-start.2 = (bf16[512,4096]{1,0:T(8,128)(2,1)}, bf16[512,4096]{1,0:T(8,128)(2,1)}, u32[]{:S(2)}, u32[]{:S(2)}) collective-permute-start(bf16[512,4096]{1,0:T(8,128)(2,1)} %maximum_select_fusion.1), channel_id=1, source_target_pairs={{0,4},{1,5},{2,6},{3,7},{4,0},{5,1},{6,2},{7,3},{8,12},{9,13},{10,... | collective-permute-start | bytes 12582920 | tf_op jit(solution)/shard_map/ppermute | solution.py:117
  996.2 56.0 %copy-start.4 = (s32[4096]{0:T(1024)S(1)}, s32[4096]{0:T(1024)}, u32[]{:S(2)}) copy-start(s32[4096]{0:T(1024)} %get-tuple-element.474) | copy-start | bytes 49156
  1052.2 23.0 %copy-start.3 = (s32[4096]{0:T(1024)S(1)}, s32[4096]{0:T(1024)}, u32[]{:S(2)}) copy-start(s32[4096]{0:T(1024)} %copy-done.2) | copy-start | bytes 49156
Sparse Core Ops, SparseCore 0:
  466.1 158.9 reduce-scatter.1
  626.7 33.4 all-gather.6
  674.8 34.4 all-gather.8
